TPU v7x, 32 devices: a whole 2x2x4 slice. The times are simulated.
32 devices in a mesh: dp: 4 (over y, x), fsdp: 8 (over z, core).
Axes of the slice: x: 2, y: 2, z: 4, core: 2. Of those that a mesh axis runs over, the one named last changes fastest.
Arguments:
- token_ids: int32 [32, 128], P(('dp', 'fsdp')), may hold values from 0 to 8191
- target_ids: int32 [32, 128], P(('dp', 'fsdp')), may hold values from 0 to 8191
- domain_ids: int32 [32, 1], P(('dp', 'fsdp')), may hold values from 0 to 21
- in_embed: bfloat16 [8192, 128], P('fsdp'), may hold values from -6 to 6
- out_embed: bfloat16 [8192, 128], P('fsdp'), may hold values from -42.426407 to 42.426407
- ref_norm1: bfloat16 [128], P('fsdp'), may hold values from 0.5 to 1.5
- ref_gate: bfloat16 [512, 128], P('fsdp'), may hold values from -0.5 to 0.5
- ref_up: bfloat16 [512, 128], P('fsdp'), may hold values from -0.5 to 0.5
- ref_down: bfloat16 [512, 128], P('fsdp'), may hold values from -0.25 to 0.25
- ref_norm2: bfloat16 [128], P('fsdp'), may hold values from 0.5 to 1.5
- prx_norm1: bfloat16 [128], P('fsdp'), may hold values from 0.5 to 1.5
- prx_gate: bfloat16 [512, 128], P('fsdp'), may hold values from -0.5 to 0.5
- prx_up: bfloat16 [512, 128], P('fsdp'), may hold values from -0.5 to 0.5
- prx_down: bfloat16 [512, 128], P('fsdp'), may hold values from -0.25 to 0.25
- prx_norm2: bfloat16 [128], P('fsdp'), may hold values from 0.5 to 1.5
- alpha_prev: float32 [22], replicated, may hold values from 0.01 to 0.1
Outputs:
- alpha_new: float32 [22], replicated
- grad_gate: float32 [512, 128], P('fsdp')
- grad_up: float32 [512, 128], P('fsdp')
- grad_down: float32 [512, 128], P('fsdp')
Inputs may be any that keep to these rules, and one draw needn't show every extreme that they name: `domain_ids`: every one of the 22 domains is the domain of at least one row.
All inputs are finite; a program needn't handle non-finite values.
Results may differ from a plain program's by a relative error of at most 0.0075.
The roundings to bfloat16 on the way count: a program that leaves them out, or rounds other values in their place, can miss the bound.
Values may be sent and summed in bfloat16 or wider, within the bound.
No kernel may reach another device: no remote copies, remote signals or barrier semaphores. Data moves between devices by JAX's collectives and lax.ppermute only.
A program may use at most 64 MiB of HBM per device.

v0:
```python
import math
import jax
import jax.numpy as jnp
from jax import lax
from jax.sharding import PartitionSpec as P

EPSILON = 1e-05
SMOOTHING = 0.001


def combined_all(value, axis, join):
    pieces = jax.tree.map(lambda part: lax.all_gather(part, axis), value)
    head = jax.tree.map(lambda part: part[0], pieces)
    tail = jax.tree.map(lambda part: part[1:], pieces)
    running, _ = lax.scan(lambda running, piece: (join(running, piece), None), head, tail)
    return running


def rms_scale(values):
    return lax.rsqrt(jnp.mean(values * values, axis=1, keepdims=True) + EPSILON)


def contract_last(left_side, right_side):
    return lax.dot_general(
        left_side, right_side, (((1,), (1,)), ((), ())), preferred_element_type=jnp.float32
    )


def contract_first(left_side, right_side):
    return lax.dot_general(
        left_side, right_side, (((0,), (0,)), ((), ())), preferred_element_type=jnp.float32
    )


def feed_forward(embedded, normed, weights):
    gate_weight, up_weight, down_weight, norm_first, norm_second = weights
    first_in = (normed * norm_first.astype(jnp.float32)).astype(jnp.bfloat16)
    gate_act = contract_last(first_in, gate_weight)
    up_act = contract_last(first_in, up_weight)
    hidden = (gate_act * jax.nn.sigmoid(gate_act) * up_act).astype(jnp.bfloat16)
    stream = embedded + jnp.dot(hidden, down_weight, preferred_element_type=jnp.float32)
    second_scale = rms_scale(stream)
    unit_stream = stream * second_scale
    second_in = (unit_stream * norm_second.astype(jnp.float32)).astype(jnp.bfloat16)
    return (second_in, (first_in, gate_act, up_act, hidden, second_scale, unit_stream))


def gather_layer(gate_shard, up_shard, down_shard, norm_first, norm_second):
    return (
        lax.all_gather(gate_shard, "fsdp", axis=0, tiled=True),
        lax.all_gather(up_shard, "fsdp", axis=0, tiled=True),
        lax.all_gather(down_shard, "fsdp", axis=0, tiled=True),
        lax.all_gather(norm_first, "fsdp", axis=0, tiled=True),
        lax.all_gather(norm_second, "fsdp", axis=0, tiled=True),
    )


def shard_stats(second_in, table, local_target):
    row_total = second_in.shape[0]
    block_rows = math.gcd(row_total, 512)
    block_count = row_total // block_rows
    column_range = jnp.arange(table.shape[0], dtype=jnp.int32)

    def shard_one_block(block):
        inputs, targets = block
        logits = contract_last(inputs, table)
        top_logit = jnp.max(logits, axis=1)
        exp_total = jnp.sum(jnp.exp(logits - top_logit[:, None]), axis=1)
        picked = jnp.sum(jnp.where(targets[:, None] == column_range[None, :], logits, 0.0), axis=1)
        return (top_logit, exp_total, picked)

    results = lax.map(
        shard_one_block,
        (
            second_in.reshape(block_count, block_rows, -1),
            local_target.reshape(block_count, block_rows),
        ),
    )
    return tuple((item.reshape(row_total) for item in results))


def combine_stats(first, second):
    merged = []
    for offset in range(0, len(first), 3):
        top_first, total_first, pick_first = (first[offset], first[offset + 1], first[offset + 2])
        top_second, total_second, pick_second = (
            second[offset],
            second[offset + 1],
            second[offset + 2],
        )
        top_logit = jnp.maximum(top_first, top_second)
        exp_total = total_first * jnp.exp(top_first - top_logit) + total_second * jnp.exp(
            top_second - top_logit
        )
        merged = merged + [top_logit, exp_total, pick_first + pick_second]
    return tuple(merged)


def body(
    token_ids,
    target_ids,
    domain_ids,
    in_embed,
    out_embed,
    ref_norm1,
    ref_gate,
    ref_up,
    ref_down,
    ref_norm2,
    prx_norm1,
    prx_gate,
    prx_up,
    prx_down,
    prx_norm2,
    alpha_prev,
):
    domain_total = alpha_prev.shape[0]
    rows_here, seq_len = token_ids.shape
    per_device = rows_here * seq_len
    vocab_here = in_embed.shape[0]
    width = in_embed.shape[1]
    fsdp_size = lax.axis_size("fsdp")
    vocab_start = lax.axis_index("fsdp") * vocab_here
    all_tokens, all_targets, all_domains = (
        lax.all_gather(token_ids, "fsdp", axis=0, tiled=True),
        lax.all_gather(target_ids, "fsdp", axis=0, tiled=True),
        lax.all_gather(domain_ids, "fsdp", axis=0, tiled=True),
    )
    token_local = all_tokens.reshape(-1) - vocab_start
    target_local = all_targets.reshape(-1) - vocab_start
    domain_flat = jnp.repeat(all_domains[:, 0], seq_len)
    domain_range = jnp.arange(domain_total, dtype=jnp.int32)
    dom_hits = (domain_flat[:, None] == domain_range[None, :]).astype(jnp.float32)
    inside = ((token_local >= 0) & (token_local < vocab_here)).astype(jnp.float32)
    picked_rows = (
        jnp.take(in_embed, jnp.clip(token_local, 0, vocab_here - 1), axis=0).astype(jnp.float32)
        * inside[:, None]
    )
    ref_weights = gather_layer(ref_gate, ref_up, ref_down, ref_norm1, ref_norm2)
    prx_weights = gather_layer(prx_gate, prx_up, prx_down, prx_norm1, prx_norm2)
    embedded = lax.psum_scatter(
        picked_rows.astype(jnp.bfloat16), "fsdp", scatter_dimension=0, tiled=True
    ).astype(jnp.float32)
    normed = embedded * rms_scale(embedded)
    ref_own = feed_forward(embedded, normed, ref_weights)[0]
    prx_own, saved_state = feed_forward(embedded, normed, prx_weights)
    ref_group, prx_group = (
        lax.all_gather(ref_own, "fsdp", axis=0, tiled=True),
        lax.all_gather(prx_own, "fsdp", axis=0, tiled=True),
    )
    ref_top, ref_sum, ref_pick = shard_stats(ref_group, out_embed, target_local)
    prx_top, prx_sum, prx_pick = shard_stats(prx_group, out_embed, target_local)
    merged = combined_all(
        (ref_top, ref_sum, ref_pick, prx_top, prx_sum, prx_pick), "fsdp", combine_stats
    )
    ref_loss = merged[0] + jnp.log(merged[1]) - merged[2]
    prx_total = merged[3] + jnp.log(merged[4])
    excess = jnp.maximum(prx_total - merged[5] - ref_loss, 0.0)
    total_sums, domain_counts = lax.psum(
        (jnp.sum(dom_hits * excess[:, None], axis=0), jnp.sum(dom_hits, axis=0)), "dp"
    )
    softmax_mix = jax.nn.softmax(jnp.log(alpha_prev) + total_sums / domain_counts)
    alpha_new = (1.0 - SMOOTHING) * softmax_mix + SMOOTHING / domain_total
    device_total = per_device * lax.axis_size("dp") * fsdp_size
    token_ratio = math.sqrt(device_total) * alpha_new / domain_counts
    token_weight = jnp.sum(dom_hits * token_ratio[None, :], axis=1)
    column_range = jnp.arange(vocab_here, dtype=jnp.int32)
    block_rows = math.gcd(per_device * lax.axis_size("fsdp"), 512)
    block_count = per_device * lax.axis_size("fsdp") // block_rows
    inputs = prx_group.reshape(block_count, block_rows, -1)
    totals = prx_total.reshape(block_count, block_rows)
    weights = token_weight.reshape(block_count, block_rows)
    targets = target_local.reshape(block_count, block_rows)

    def head_one_block(block):
        block_in, block_total, block_weight, block_target = block
        logits = contract_last(block_in, out_embed)
        probs = jnp.exp(logits - block_total[:, None])
        hits = (block_target[:, None] == column_range[None, :]).astype(jnp.float32)
        d_logits = (block_weight[:, None] * (probs - hits)).astype(jnp.bfloat16)
        return jnp.dot(d_logits, out_embed, preferred_element_type=jnp.float32)

    d_second = lax.psum_scatter(
        lax.map(head_one_block, (inputs, totals, weights, targets)).reshape(
            per_device * lax.axis_size("fsdp"), -1
        ),
        "fsdp",
        scatter_dimension=0,
        tiled=True,
    )
    first_in, gate_act, up_act, hidden, second_scale, unit_stream = saved_state
    d_unit = d_second * prx_weights[4].astype(jnp.float32)
    d_branch = (
        second_scale
        * (d_unit - unit_stream * jnp.mean(d_unit * unit_stream, axis=1, keepdims=True))
    ).astype(jnp.bfloat16)
    d_hidden = contract_last(d_branch, prx_weights[2])
    sigmoid_gate = jax.nn.sigmoid(gate_act)
    d_gate = (d_hidden * up_act * sigmoid_gate * (1.0 + gate_act * (1.0 - sigmoid_gate))).astype(
        jnp.bfloat16
    )
    d_up = (d_hidden * gate_act * sigmoid_gate).astype(jnp.bfloat16)
    partial_grad = jnp.concatenate(
        [
            contract_first(d_gate, first_in),
            contract_first(d_up, first_in),
            contract_first(hidden, d_branch),
        ],
        axis=1,
    )
    rounded = lax.optimization_barrier(partial_grad.astype(jnp.bfloat16))
    local_grad = lax.psum_scatter(
        rounded.astype(jnp.float32).astype(jnp.bfloat16), "fsdp", scatter_dimension=0, tiled=True
    ).astype(jnp.float32)
    grad_shard = lax.psum(local_grad, "dp")
    return (
        alpha_new,
        grad_shard[:, :width],
        grad_shard[:, width : 2 * width],
        grad_shard[:, 2 * width :],
    )


def solution(mesh):
    placed = (
        P(("dp", "fsdp"), None),
        P(("dp", "fsdp"), None),
        P(("dp", "fsdp"), None),
        P("fsdp", None),
        P("fsdp", None),
        P("fsdp"),
        P("fsdp", None),
        P("fsdp", None),
        P("fsdp", None),
        P("fsdp"),
        P("fsdp"),
        P("fsdp", None),
        P("fsdp", None),
        P("fsdp", None),
        P("fsdp"),
        P(),
    )
    return jax.shard_map(
        body,
        mesh=mesh,
        in_specs=placed,
        out_specs=(P(), P("fsdp", None), P("fsdp", None), P("fsdp", None)),
        check_vma=False,
    )
```

profile of v0, /device:TPU:0, one launch (start us, length us, event | category | flops | bytes accessed | tf_op | source)
XLA Modules:
  0.0 369.3 jit_solution(6620996398305857346)
XLA Ops:
  7.4 13.7 %all-gather = s32[8,1,128]{2,1,0:T(1,128)S(1)} all-gather(s32[1,1,128]{2,1,0:T(1,128)} %bitcast.177), channel_id=1, replica_groups=mesh['dp'=4,'fsdp'=8] {'fsdp'}, dimensions={0}, use_global_device_ids=true | all-gather | bytes 4608 | tf_op jit(solution)/shard_map/all_gather | solution.py:125
  21.1 3.2 gather_fusion
  26.1 8.6 %all-gather.1 = s32[8,1,128]{2,1,0:T(1,128)S(1)} all-gather(s32[1,1,128]{2,1,0:T(1,128)S(1)} %bitcast.178), channel_id=1, replica_groups=mesh['dp'=4,'fsdp'=8] {'fsdp'}, dimensions={0}, use_global_device_ids=true | all-gather | bytes 4608 | tf_op jit(solution)/shard_map/all_gather | solution.py:126
  36.1 14.0 %all_gather.78 = bf16[512,128]{1,0:T(8,128)(2,1)S(1)} all-gather(bf16[64,128]{1,0:T(8,128)(2,1)S(1)} %copy-done.2), channel_id=1, replica_groups=mesh['dp'=4,'fsdp'=8] {'fsdp'}, dimensions={0}, use_global_device_ids=true | all-gather | bytes 147456 | tf_op jit(solution)/shard_map/all_gather | solution.py:52
  50.1 7.2 %all-reduce = s32[8]{0:T(128)S(1)} all-reduce(s32[8]{0:T(128)S(1)} %bitcast_dynamic-update-slice_fusion), channel_id=1, replica_groups=mesh['dp'=4,'fsdp'=8] {'fsdp'}, use_global_device_ids=true, to_apply=%add | all-reduce | flops 8 | bytes 64
  59.0 13.9 %all-reduce.6 = (bf16[128]{0:T(256)(128)(2,1)S(1)}, bf16[128]{0:T(256)(128)(2,1)S(1)}, bf16[128]{0:T(256)(128)(2,1)S(1)}, bf16[128]{0:T(256)(128)(2,1)S(1)}) all-reduce(bf16[128]{0:T(256)(128)(2,1)S(1)} %dynamic-update-slice.1, bf16[128]{0:T(256)(128)(2,1)S(1)} %dynamic-update-slice.2, ...), channel_id=1, replica_groups=mesh['dp'=4,'fsdp'=8] {'fsdp'}, use_global_device_ids=true, to_apply=%add.1 | all-reduce | flops 512 | bytes 2048
  73.0 14.0 %all_gather.66 = bf16[512,128]{1,0:T(8,128)(2,1)S(1)} all-gather(bf16[64,128]{1,0:T(8,128)(2,1)S(1)} %copy-done.3), channel_id=1, replica_groups=mesh['dp'=4,'fsdp'=8] {'fsdp'}, dimensions={0}, use_global_device_ids=true | all-gather | bytes 147456 | tf_op jit(solution)/shard_map/all_gather | solution.py:50
  87.0 14.0 %all_gather.67 = bf16[512,128]{1,0:T(8,128)(2,1)S(1)} all-gather(bf16[64,128]{1,0:T(8,128)(2,1)S(1)} %copy-done.4), channel_id=1, replica_groups=mesh['dp'=4,'fsdp'=8] {'fsdp'}, dimensions={0}, use_global_device_ids=true | all-gather | bytes 147456 | tf_op jit(solution)/shard_map/all_gather | solution.py:51
  101.0 14.0 %all_gather.68 = bf16[512,128]{1,0:T(8,128)(2,1)S(1)} all-gather(bf16[64,128]{1,0:T(8,128)(2,1)S(1)} %copy-done.5), channel_id=1, replica_groups=mesh['dp'=4,'fsdp'=8] {'fsdp'}, dimensions={0}, use_global_device_ids=true | all-gather | bytes 147456 | tf_op jit(solution)/shard_map/all_gather | solution.py:52
  114.9 14.0 %all_gather.76 = bf16[512,128]{1,0:T(8,128)(2,1)S(1)} all-gather(bf16[64,128]{1,0:T(8,128)(2,1)S(1)} %copy-done.6), channel_id=1, replica_groups=mesh['dp'=4,'fsdp'=8] {'fsdp'}, dimensions={0}, use_global_device_ids=true | all-gather | bytes 147456 | tf_op jit(solution)/shard_map/all_gather | solution.py:50
  128.9 14.0 %all_gather.77 = bf16[512,128]{1,0:T(8,128)(2,1)S(1)} all-gather(bf16[64,128]{1,0:T(8,128)(2,1)S(1)} %copy-done.7), channel_id=1, replica_groups=mesh['dp'=4,'fsdp'=8] {'fsdp'}, dimensions={0}, use_global_device_ids=true | all-gather | bytes 147456 | tf_op jit(solution)/shard_map/all_gather | solution.py:51
  144.7 13.1 %all_gather.70 = bf16[1024,128]{0,1:T(8,128)(2,1)S(1)} all-gather(bf16[128,128]{0,1:T(8,128)(2,1)S(1)} %multiply_convert_fusion.9), channel_id=1, replica_groups=mesh['dp'=4,'fsdp'=8] {'fsdp'}, dimensions={0}, use_global_device_ids=true | all-gather | bytes 294912 | tf_op jit(solution)/shard_map/all_gather | solution.py:148
  161.0 14.0 %all-gather.3 = f32[8,1,1024]{2,1,0:T(1,128)S(1)} all-gather(f32[1,1,1024]{2,1,0:T(1,128)S(1)} %reshape.171), channel_id=1, replica_groups=mesh['dp'=4,'fsdp'=8] {'fsdp'}, dimensions={0}, use_global_device_ids=true | all-gather | bytes 36864 | tf_op jit(solution)/shard_map/all_gather | solution.py:12
  175.1 14.0 %all-gather.2 = f32[8,1,1024]{2,1,0:T(1,128)S(1)} all-gather(f32[1,1,1024]{2,1,0:T(1,128)S(1)} %reshape.169), channel_id=1, replica_groups=mesh['dp'=4,'fsdp'=8] {'fsdp'}, dimensions={0}, use_global_device_ids=true | all-gather | bytes 36864 | tf_op jit(solution)/shard_map/all_gather | solution.py:12
  189.1 14.0 %all-gather.4 = f32[8,1,1024]{2,1,0:T(1,128)S(1)} all-gather(f32[1,1,1024]{2,1,0:T(1,128)S(1)} %reshape.173), channel_id=1, replica_groups=mesh['dp'=4,'fsdp'=8] {'fsdp'}, dimensions={0}, use_global_device_ids=true | all-gather | bytes 36864 | tf_op jit(solution)/shard_map/all_gather | solution.py:12
  204.0 13.3 %all_gather.80 = bf16[1024,128]{0,1:T(8,128)(2,1)S(1)} all-gather(bf16[128,128]{0,1:T(8,128)(2,1)S(1)} %multiply_convert_fusion.8), channel_id=1, replica_groups=mesh['dp'=4,'fsdp'=8] {'fsdp'}, dimensions={0}, use_global_device_ids=true | all-gather | bytes 294912 | tf_op jit(solution)/shard_map/all_gather | solution.py:149
  217.5 3.0 while.63
  220.5 14.0 %all-gather.6 = f32[8,1,1024]{2,1,0:T(1,128)S(1)} all-gather(f32[1,1,1024]{2,1,0:T(1,128)S(1)} %reshape.177), channel_id=1, replica_groups=mesh['dp'=4,'fsdp'=8] {'fsdp'}, dimensions={0}, use_global_device_ids=true | all-gather | bytes 36864 | tf_op jit(solution)/shard_map/all_gather | solution.py:12
  234.5 14.0 %all-gather.5 = f32[8,1,1024]{2,1,0:T(1,128)S(1)} all-gather(f32[1,1,1024]{2,1,0:T(1,128)S(1)} %reshape.175), channel_id=1, replica_groups=mesh['dp'=4,'fsdp'=8] {'fsdp'}, dimensions={0}, use_global_device_ids=true | all-gather | bytes 36864 | tf_op jit(solution)/shard_map/all_gather | solution.py:12
  248.6 14.0 %all-gather.7 = f32[8,1,1024]{2,1,0:T(1,128)S(1)} all-gather(f32[1,1,1024]{2,1,0:T(1,128)S(1)} %reshape.179), channel_id=1, replica_groups=mesh['dp'=4,'fsdp'=8] {'fsdp'}, dimensions={0}, use_global_device_ids=true | all-gather | bytes 36864 | tf_op jit(solution)/shard_map/all_gather | solution.py:12
  263.9 9.9 %all-reduce.5 = (f32[22]{0:T(128)S(1)}, f32[22]{0:T(128)S(1)}) all-reduce(f32[22]{0:T(128)S(1)} %get-tuple-element.346, f32[22]{0:T(128)S(1)} %get-tuple-element.347), channel_id=1, replica_groups=mesh['dp'=4,'fsdp'=8] {'dp'}, use_global_device_ids=true, to_apply=%region_19.20 | all-reduce | flops 44 | bytes 352 | tf_op jit(solution)/shard_map/psum | solution.py:159
  280.5 27.4 %reduce-scatter.8.cloned.1.call-done = f32[128,128]{0,1:T(8,128)} async-done(((f32[1024,128]{0,1:T(8,128)}), f32[128,128]{0,1:T(8,128)}) %reduce-scatter.8.cloned.1.call-update) | async-done | bytes 65552 | tf_op jit(solution)/shard_map/reduce_scatter | solution.py:183
  311.7 29.0 %reduce-scatter.12.cloned.1.call-done = bf16[64,384]{1,0:T(8,128)(2,1)} async-done(((bf16[512,384]{1,0:T(8,128)(2,1)}), bf16[64,384]{1,0:T(8,128)(2,1)}) %reduce-scatter.12.cloned.1.call-update) | async-done | bytes 49168
  341.6 19.0 %all-reduce.8 = f32[64,384]{0,1:T(8,128)S(1)} all-reduce(bf16[64,384]{0,1:T(8,128)(2,1)S(1)} %copy.55), channel_id=1, replica_groups=mesh['dp'=4,'fsdp'=8] {'dp'}, use_global_device_ids=true, to_apply=%region_28.29 | all-reduce | flops 24576 | bytes 147456 | tf_op jit(solution)/shard_map/psum | solution.py:215
  (217 shorter events, 32.5 us)
Async XLA Ops:
  7.2 13.9 %copy-start = (bf16[1024,128]{1,0:T(8,128)(2,1)S(1)}, bf16[1024,128]{1,0:T(8,128)(2,1)}, u32[]{:S(2)}) copy-start(bf16[1024,128]{1,0:T(8,128)(2,1)} %param.27) | copy-start | bytes 786436
  7.2 27.6 %copy-start.14 = (u32[32]{0:T(128)S(1)}, u32[32]{0:T(128)}, u32[]{:S(2)}) copy-start(u32[32]{0:T(128)} %constant.110) | copy-start | bytes 388
  7.2 18.9 %copy-start.8 = (s32[1,128]{1,0:T(1,128)S(1)}, s32[1,128]{1,0:T(1,128)}, u32[]{:S(2)}) copy-start(s32[1,128]{1,0:T(1,128)} %param.25) | copy-start | bytes 1540
  7.2 28.9 %copy-start.2 = (bf16[64,128]{1,0:T(8,128)(2,1)S(1)}, bf16[64,128]{1,0:T(8,128)(2,1)}, u32[]{:S(2)}) copy-start(bf16[64,128]{1,0:T(8,128)(2,1)} %param.37) | copy-start | bytes 49156
  7.2 50.8 %copy-start.10 = (bf16[16]{0:T(256)(128)(2,1)S(1)}, bf16[16]{0:T(256)(128)(2,1)}, u32[]{:S(2)}) copy-start(bf16[16]{0:T(256)(128)(2,1)} %param.34) | copy-start | bytes 100
  7.2 51.1 %copy-start.11 = (bf16[16]{0:T(256)(128)(2,1)S(1)}, bf16[16]{0:T(256)(128)(2,1)}, u32[]{:S(2)}) copy-start(bf16[16]{0:T(256)(128)(2,1)} %param.33) | copy-start | bytes 100
  7.2 51.3 %copy-start.12 = (bf16[16]{0:T(256)(128)(2,1)S(1)}, bf16[16]{0:T(256)(128)(2,1)}, u32[]{:S(2)}) copy-start(bf16[16]{0:T(256)(128)(2,1)} %param.29) | copy-start | bytes 100
  7.2 51.5 %copy-start.13 = (bf16[16]{0:T(256)(128)(2,1)S(1)}, bf16[16]{0:T(256)(128)(2,1)}, u32[]{:S(2)}) copy-start(bf16[16]{0:T(256)(128)(2,1)} %param.38) | copy-start | bytes 100
  7.3 65.8 %copy-start.3 = (bf16[64,128]{1,0:T(8,128)(2,1)S(1)}, bf16[64,128]{1,0:T(8,128)(2,1)}, u32[]{:S(2)}) copy-start(bf16[64,128]{1,0:T(8,128)(2,1)} %param.30) | copy-start | bytes 49156
  7.3 79.7 %copy-start.4 = (bf16[64,128]{1,0:T(8,128)(2,1)S(1)}, bf16[64,128]{1,0:T(8,128)(2,1)}, u32[]{:S(2)}) copy-start(bf16[64,128]{1,0:T(8,128)(2,1)} %param.31) | copy-start | bytes 49156
  7.3 93.7 %copy-start.5 = (bf16[64,128]{1,0:T(8,128)(2,1)S(1)}, bf16[64,128]{1,0:T(8,128)(2,1)}, u32[]{:S(2)}) copy-start(bf16[64,128]{1,0:T(8,128)(2,1)} %param.32) | copy-start | bytes 49156
  7.3 107.6 %copy-start.6 = (bf16[64,128]{1,0:T(8,128)(2,1)S(1)}, bf16[64,128]{1,0:T(8,128)(2,1)}, u32[]{:S(2)}) copy-start(bf16[64,128]{1,0:T(8,128)(2,1)} %param.35) | copy-start | bytes 49156
  7.3 121.6 %copy-start.7 = (bf16[64,128]{1,0:T(8,128)(2,1)S(1)}, bf16[64,128]{1,0:T(8,128)(2,1)}, u32[]{:S(2)}) copy-start(bf16[64,128]{1,0:T(8,128)(2,1)} %param.36) | copy-start | bytes 49156
  7.3 135.6 %reduce-scatter.10.cloned.1.call-start = ((), (), s32[]{:S(2)}) async-start(), calls=%async_computation.4 | async-start | bytes 294912
  25.4 132.7 %copy-start.1 = (bf16[1024,128]{1,0:T(8,128)(2,1)S(1)}, bf16[1024,128]{1,0:T(8,128)(2,1)}, u32[]{:S(2)}) copy-start(bf16[1024,128]{1,0:T(8,128)(2,1)} %param.28) | copy-start | bytes 786436
  25.4 282.5 %reduce-scatter.8.cloned.1.call-start = ((), (), s32[]{:S(2)}) async-start(), calls=%async_computation.3 | async-start | bytes 589824 | tf_op jit(solution)/shard_map/reduce_scatter | solution.py:183
  217.5 56.4 %copy-start.9 = (f32[22]{0:T(128)S(1)}, f32[22]{0:T(128)}, u32[]{:S(2)}) copy-start(f32[22]{0:T(128)} %param.39) | copy-start | bytes 268
  280.5 60.2 %reduce-scatter.12.cloned.1.call-start = ((), (), s32[]{:S(2)}) async-start(), calls=%async_computation.5 | async-start | bytes 442368
Sparse Core Ops, SparseCore 0:
  25.5 28.6 reduce-scatter.9
  280.6 27.2 reduce-scatter.7
  311.8 28.8 reduce-scatter.11
where the time goes:
time: 370 us; the launch traced here: 369 us
  blocking collectives  267 us (72%)
  waiting for transfers between devices  56.4 us (15%)
  between operations  15.6 us (4%)
  local copies, waits for them, and re-layouts  12.9 us (3%)
  other arithmetic  10.5 us (3%)
  matrix products  6.23 us (2%)
    all_gather x6, blocking collectives, combined_all(): pieces = jax.tree.map(lambda part: lax.all_gather(part, axis), value)  84 us
    unnamed x5, waiting for transfers between devices  29.1 us
    all_gather x2, blocking collectives, gather_layer(): lax.all_gather(down_shard, 'fsdp', axis=0, tiled=True)  28 us
    all_gather x2, blocking collectives, gather_layer(): lax.all_gather(gate_shard, 'fsdp', axis=0, tiled=True)  27.9 us
    all_gather x2, blocking collectives, gather_layer(): lax.all_gather(up_shard, 'fsdp', axis=0, tiled=True)  27.9 us
    reduce_scatter x1, waiting for transfers between devices, body(): lax.psum_scatter(lax.map(head_one_block, (inputs, totals, weights, target...  27.4 us
    unnamed x2, blocking collectives  21.2 us
    psum x1, blocking collectives, body(): grad_shard = lax.psum(local_grad, 'dp')  19 us
  transfers between devices with their start and end apart: 3, of which 2 were waited for; matrix products, arithmetic and copies ran while one was open for 1% of the time, Pallas kernels for 0%

commit v1 on v0

--- a/solution.py
+++ b/solution.py
@@ -212,7 +212,7 @@
     local_grad = lax.psum_scatter(
         rounded.astype(jnp.float32).astype(jnp.bfloat16), "fsdp", scatter_dimension=0, tiled=True
     ).astype(jnp.float32)
-    grad_shard = lax.psum(local_grad, "dp")
+    grad_shard = jnp.sum(lax.all_gather(local_grad, "dp"), axis=0)
     return (
         alpha_new,
         grad_shard[:, :width],

time: 370 us -> 369 us (level)
  blocking collectives: 267 us -> 258 us
    reduce_scatter x0 -> x1, waiting for transfers between devices: none -> 29.1 us  [body(): lax.psum_scatter(rounded.astype(jnp.float32).astype(jnp.bfloat16), 'fsdp'...]
    unnamed x5 -> x4, waiting for transfers between devices: 29.1 us -> 0.05 us
    psum x1 -> x0, blocking collectives: 19 us -> none  [body(): grad_shard = lax.psum(local_grad, 'dp')]
    all_gather x0 -> x1, blocking collectives: none -> 9.47 us  [body(): grad_shard = jnp.sum(lax.all_gather(local_grad, 'dp'), axis=0)]
    unnamed x61 -> x71, local copies, waits for them, and re-layouts: 7.57 us -> 6.84 us
where the time goes in v1:
time: 369 us; the launch traced here: 368 us
  blocking collectives  258 us (70%)
  waiting for transfers between devices  56.5 us (15%)
  local copies, waits for them, and re-layouts  15.7 us (4%)
  between operations  15.7 us (4%)
  other arithmetic  12 us (3%)
  matrix products  9.23 us (3%)
    all_gather x6, blocking collectives, combined_all(): pieces = jax.tree.map(lambda part: lax.all_gather(part, axis), value)  84 us
    reduce_scatter x1, waiting for transfers between devices, body(): lax.psum_scatter(rounded.astype(jnp.float32).astype(jnp.bfloat16), 'fsdp'...  29.1 us
    all_gather x2, blocking collectives, gather_layer(): lax.all_gather(up_shard, 'fsdp', axis=0, tiled=True)  29 us
    all_gather x2, blocking collectives, gather_layer(): lax.all_gather(down_shard, 'fsdp', axis=0, tiled=True)  28 us
    all_gather x2, blocking collectives, gather_layer(): lax.all_gather(gate_shard, 'fsdp', axis=0, tiled=True)  27.9 us
    reduce_scatter x1, waiting for transfers between devices, body(): lax.psum_scatter(lax.map(head_one_block, (inputs, totals, weights, target...  27.4 us
    unnamed x2, blocking collectives  21.2 us
    all_gather x1, blocking collectives, body(): lax.all_gather(token_ids, 'fsdp', axis=0, tiled=True)  13.7 us
  transfers between devices with their start and end apart: 3, of which 2 were waited for; matrix products, arithmetic and copies ran while one was open for 1% of the time, Pallas kernels for 0%

profile of v1, /device:TPU:0, one launch (start us, length us, event | category | flops | bytes accessed | tf_op | source)
XLA Modules:
  0.0 368.1 jit_solution(3586796388426275132)
XLA Ops:
  7.4 13.7 %all-gather.1 = s32[8,1,128]{2,1,0:T(1,128)S(1)} all-gather(s32[1,1,128]{2,1,0:T(1,128)} %bitcast.179), channel_id=1, replica_groups=mesh['dp'=4,'fsdp'=8] {'fsdp'}, dimensions={0}, use_global_device_ids=true | all-gather | bytes 4608 | tf_op jit(solution)/shard_map/all_gather | solution.py:125
  21.1 3.2 gather_fusion
  26.1 8.6 %all-gather.2 = s32[8,1,128]{2,1,0:T(1,128)S(1)} all-gather(s32[1,1,128]{2,1,0:T(1,128)S(1)} %bitcast.180), channel_id=1, replica_groups=mesh['dp'=4,'fsdp'=8] {'fsdp'}, dimensions={0}, use_global_device_ids=true | all-gather | bytes 4608 | tf_op jit(solution)/shard_map/all_gather | solution.py:126
  36.1 14.0 %all_gather.77 = bf16[512,128]{1,0:T(8,128)(2,1)S(1)} all-gather(bf16[64,128]{1,0:T(8,128)(2,1)S(1)} %copy-done.3), channel_id=1, replica_groups=mesh['dp'=4,'fsdp'=8] {'fsdp'}, dimensions={0}, use_global_device_ids=true | all-gather | bytes 147456 | tf_op jit(solution)/shard_map/all_gather | solution.py:52
  50.1 7.2 %all-reduce = s32[8]{0:T(128)S(1)} all-reduce(s32[8]{0:T(128)S(1)} %bitcast_dynamic-update-slice_fusion), channel_id=1, replica_groups=mesh['dp'=4,'fsdp'=8] {'fsdp'}, use_global_device_ids=true, to_apply=%add | all-reduce | flops 8 | bytes 64
  59.0 13.9 %all-reduce.6 = (bf16[128]{0:T(256)(128)(2,1)S(1)}, bf16[128]{0:T(256)(128)(2,1)S(1)}, bf16[128]{0:T(256)(128)(2,1)S(1)}, bf16[128]{0:T(256)(128)(2,1)S(1)}) all-reduce(bf16[128]{0:T(256)(128)(2,1)S(1)} %dynamic-update-slice.1, bf16[128]{0:T(256)(128)(2,1)S(1)} %dynamic-update-slice.2, ...), channel_id=1, replica_groups=mesh['dp'=4,'fsdp'=8] {'fsdp'}, use_global_device_ids=true, to_apply=%add.1 | all-reduce | flops 512 | bytes 2048
  73.0 14.0 %all_gather.76 = bf16[512,128]{1,0:T(8,128)(2,1)S(1)} all-gather(bf16[64,128]{1,0:T(8,128)(2,1)S(1)} %copy-done.4), channel_id=1, replica_groups=mesh['dp'=4,'fsdp'=8] {'fsdp'}, dimensions={0}, use_global_device_ids=true | all-gather | bytes 147456 | tf_op jit(solution)/shard_map/all_gather | solution.py:51
  87.0 14.0 %all_gather.75 = bf16[512,128]{1,0:T(8,128)(2,1)S(1)} all-gather(bf16[64,128]{1,0:T(8,128)(2,1)S(1)} %copy-done.5), channel_id=1, replica_groups=mesh['dp'=4,'fsdp'=8] {'fsdp'}, dimensions={0}, use_global_device_ids=true | all-gather | bytes 147456 | tf_op jit(solution)/shard_map/all_gather | solution.py:50
  101.0 14.0 %all_gather.85 = bf16[512,128]{1,0:T(8,128)(2,1)S(1)} all-gather(bf16[64,128]{1,0:T(8,128)(2,1)S(1)} %copy-done.6), channel_id=1, replica_groups=mesh['dp'=4,'fsdp'=8] {'fsdp'}, dimensions={0}, use_global_device_ids=true | all-gather | bytes 147456 | tf_op jit(solution)/shard_map/all_gather | solution.py:50
  115.0 15.0 %all_gather.86 = bf16[512,128]{1,0:T(8,128)(2,1)} all-gather(bf16[64,128]{1,0:T(8,128)(2,1)S(1)} %copy-done.7), channel_id=1, replica_groups=mesh['dp'=4,'fsdp'=8] {'fsdp'}, dimensions={0}, use_global_device_ids=true | all-gather | bytes 147456 | tf_op jit(solution)/shard_map/all_gather | solution.py:51
  130.0 14.0 %all_gather.87 = bf16[512,128]{1,0:T(8,128)(2,1)S(1)} all-gather(bf16[64,128]{1,0:T(8,128)(2,1)S(1)} %copy-done.8), channel_id=1, replica_groups=mesh['dp'=4,'fsdp'=8] {'fsdp'}, dimensions={0}, use_global_device_ids=true | all-gather | bytes 147456 | tf_op jit(solution)/shard_map/all_gather | solution.py:52
  145.8 13.1 %all_gather.79 = bf16[1024,128]{0,1:T(8,128)(2,1)S(1)} all-gather(bf16[128,128]{0,1:T(8,128)(2,1)S(1)} %multiply_convert_fusion.9), channel_id=1, replica_groups=mesh['dp'=4,'fsdp'=8] {'fsdp'}, dimensions={0}, use_global_device_ids=true | all-gather | bytes 294912 | tf_op jit(solution)/shard_map/all_gather | solution.py:148
  162.1 14.0 %all-gather.3 = f32[8,1,1024]{2,1,0:T(1,128)S(1)} all-gather(f32[1,1,1024]{2,1,0:T(1,128)S(1)} %reshape.171), channel_id=1, replica_groups=mesh['dp'=4,'fsdp'=8] {'fsdp'}, dimensions={0}, use_global_device_ids=true | all-gather | bytes 36864 | tf_op jit(solution)/shard_map/all_gather | solution.py:12
  176.7 14.0 %all-gather.4 = f32[8,1,1024]{2,1,0:T(1,128)S(1)} all-gather(f32[1,1,1024]{2,1,0:T(1,128)S(1)} %reshape.173), channel_id=1, replica_groups=mesh['dp'=4,'fsdp'=8] {'fsdp'}, dimensions={0}, use_global_device_ids=true | all-gather | bytes 36864 | tf_op jit(solution)/shard_map/all_gather | solution.py:12
  191.4 14.0 %all-gather.5 = f32[8,1,1024]{2,1,0:T(1,128)S(1)} all-gather(f32[1,1,1024]{2,1,0:T(1,128)S(1)} %reshape.175), channel_id=1, replica_groups=mesh['dp'=4,'fsdp'=8] {'fsdp'}, dimensions={0}, use_global_device_ids=true | all-gather | bytes 36864 | tf_op jit(solution)/shard_map/all_gather | solution.py:12
  208.6 13.3 %all_gather.89 = bf16[1024,128]{0,1:T(8,128)(2,1)S(1)} all-gather(bf16[128,128]{0,1:T(8,128)(2,1)S(1)} %multiply_convert_fusion.8), channel_id=1, replica_groups=mesh['dp'=4,'fsdp'=8] {'fsdp'}, dimensions={0}, use_global_device_ids=true | all-gather | bytes 294912 | tf_op jit(solution)/shard_map/all_gather | solution.py:149
  225.0 14.0 %all-gather.6 = f32[8,1,1024]{2,1,0:T(1,128)S(1)} all-gather(f32[1,1,1024]{2,1,0:T(1,128)S(1)} %reshape.177), channel_id=1, replica_groups=mesh['dp'=4,'fsdp'=8] {'fsdp'}, dimensions={0}, use_global_device_ids=true | all-gather | bytes 36864 | tf_op jit(solution)/shard_map/all_gather | solution.py:12
  239.1 14.0 %all-gather.7 = f32[8,1,1024]{2,1,0:T(1,128)S(1)} all-gather(f32[1,1,1024]{2,1,0:T(1,128)S(1)} %reshape.179), channel_id=1, replica_groups=mesh['dp'=4,'fsdp'=8] {'fsdp'}, dimensions={0}, use_global_device_ids=true | all-gather | bytes 36864 | tf_op jit(solution)/shard_map/all_gather | solution.py:12
  253.1 14.0 %all-gather.8 = f32[8,1,1024]{2,1,0:T(1,128)S(1)} all-gather(f32[1,1,1024]{2,1,0:T(1,128)S(1)} %reshape.181), channel_id=1, replica_groups=mesh['dp'=4,'fsdp'=8] {'fsdp'}, dimensions={0}, use_global_device_ids=true | all-gather | bytes 36864 | tf_op jit(solution)/shard_map/all_gather | solution.py:12
  270.7 9.9 %all-reduce.5 = (f32[22]{0:T(128)S(1)}, f32[22]{0:T(128)S(1)}) all-reduce(f32[22]{0:T(128)S(1)} %get-tuple-element.377, f32[22]{0:T(128)S(1)} %get-tuple-element.376), channel_id=1, replica_groups=mesh['dp'=4,'fsdp'=8] {'dp'}, use_global_device_ids=true, to_apply=%region_17.18 | all-reduce | flops 44 | bytes 352 | tf_op jit(solution)/shard_map/psum | solution.py:159
  285.1 3.2 while.64
  290.4 27.4 %reduce-scatter.8.cloned.1.call-done = f32[128,128]{0,1:T(8,128)} async-done(((f32[1024,128]{0,1:T(8,128)}), f32[128,128]{0,1:T(8,128)}) %reduce-scatter.8.cloned.1.call-update) | async-done | bytes 65552 | tf_op jit(solution)/shard_map/reduce_scatter | solution.py:183
  321.6 29.1 %reduce-scatter.12.cloned.1.call-done = bf16[64,384]{1,0:T(8,128)(2,1)} async-done(((bf16[512,384]{1,0:T(8,128)(2,1)}), bf16[64,384]{1,0:T(8,128)(2,1)}) %reduce-scatter.12.cloned.1.call-update) | async-done | bytes 49168 | tf_op jit(solution)/shard_map/reduce_scatter | solution.py:212
  351.4 9.5 %all-gather = f32[256,384]{1,0:T(8,128)S(1)} all-gather(f32[64,384]{1,0:T(8,128)S(1)} %all_gather.96), channel_id=2, replica_groups=mesh['dp'=4,'fsdp'=8] {'dp'}, dimensions={0}, use_global_device_ids=true | all-gather | bytes 491520 | tf_op jit(solution)/shard_map/all_gather | solution.py:215
  (230 shorter events, 40.9 us)
Async XLA Ops:
  7.2 13.9 %copy-start = (bf16[1024,128]{1,0:T(8,128)(2,1)S(1)}, bf16[1024,128]{1,0:T(8,128)(2,1)}, u32[]{:S(2)}) copy-start(bf16[1024,128]{1,0:T(8,128)(2,1)} %param.27) | copy-start | bytes 786436
  7.2 27.6 %copy-start.20 = (u32[32]{0:T(128)S(1)}, u32[32]{0:T(128)}, u32[]{:S(2)}) copy-start(u32[32]{0:T(128)} %constant.110) | copy-start | bytes 388
  7.2 18.9 %copy-start.15 = (s32[1,128]{1,0:T(1,128)S(1)}, s32[1,128]{1,0:T(1,128)}, u32[]{:S(2)}) copy-start(s32[1,128]{1,0:T(1,128)} %param.25) | copy-start | bytes 1540
  7.2 28.9 %copy-start.3 = (bf16[64,128]{1,0:T(8,128)(2,1)S(1)}, bf16[64,128]{1,0:T(8,128)(2,1)}, u32[]{:S(2)}) copy-start(bf16[64,128]{1,0:T(8,128)(2,1)} %param.32) | copy-start | bytes 49156
  7.2 50.8 %copy-start.16 = (bf16[16]{0:T(256)(128)(2,1)S(1)}, bf16[16]{0:T(256)(128)(2,1)}, u32[]{:S(2)}) copy-start(bf16[16]{0:T(256)(128)(2,1)} %param.29) | copy-start | bytes 100
  7.2 51.1 %copy-start.17 = (bf16[16]{0:T(256)(128)(2,1)S(1)}, bf16[16]{0:T(256)(128)(2,1)}, u32[]{:S(2)}) copy-start(bf16[16]{0:T(256)(128)(2,1)} %param.33) | copy-start | bytes 100
  7.2 51.3 %copy-start.18 = (bf16[16]{0:T(256)(128)(2,1)S(1)}, bf16[16]{0:T(256)(128)(2,1)}, u32[]{:S(2)}) copy-start(bf16[16]{0:T(256)(128)(2,1)} %param.34) | copy-start | bytes 100
  7.2 51.5 %copy-start.19 = (bf16[16]{0:T(256)(128)(2,1)S(1)}, bf16[16]{0:T(256)(128)(2,1)}, u32[]{:S(2)}) copy-start(bf16[16]{0:T(256)(128)(2,1)} %param.38) | copy-start | bytes 100
  7.3 65.8 %copy-start.4 = (bf16[64,128]{1,0:T(8,128)(2,1)S(1)}, bf16[64,128]{1,0:T(8,128)(2,1)}, u32[]{:S(2)}) copy-start(bf16[64,128]{1,0:T(8,128)(2,1)} %param.31) | copy-start | bytes 49156
  7.3 79.7 %copy-start.5 = (bf16[64,128]{1,0:T(8,128)(2,1)S(1)}, bf16[64,128]{1,0:T(8,128)(2,1)}, u32[]{:S(2)}) copy-start(bf16[64,128]{1,0:T(8,128)(2,1)} %param.30) | copy-start | bytes 49156
  7.3 93.7 %copy-start.6 = (bf16[64,128]{1,0:T(8,128)(2,1)S(1)}, bf16[64,128]{1,0:T(8,128)(2,1)}, u32[]{:S(2)}) copy-start(bf16[64,128]{1,0:T(8,128)(2,1)} %param.35) | copy-start | bytes 49156
  7.3 107.7 %copy-start.7 = (bf16[64,128]{1,0:T(8,128)(2,1)S(1)}, bf16[64,128]{1,0:T(8,128)(2,1)}, u32[]{:S(2)}) copy-start(bf16[64,128]{1,0:T(8,128)(2,1)} %param.36) | copy-start | bytes 49156
  7.3 122.7 %copy-start.8 = (bf16[64,128]{1,0:T(8,128)(2,1)S(1)}, bf16[64,128]{1,0:T(8,128)(2,1)}, u32[]{:S(2)}) copy-start(bf16[64,128]{1,0:T(8,128)(2,1)} %param.37) | copy-start | bytes 49156
  7.3 136.7 %reduce-scatter.10.cloned.1.call-start = ((), (), s32[]{:S(2)}) async-start(), calls=%async_computation.4 | async-start | bytes 294912
  25.4 133.8 %copy-start.1 = (bf16[1024,128]{1,0:T(8,128)(2,1)S(1)}, bf16[1024,128]{1,0:T(8,128)(2,1)}, u32[]{:S(2)}) copy-start(bf16[1024,128]{1,0:T(8,128)(2,1)} %param.28) | copy-start | bytes 786436
  25.4 292.4 %reduce-scatter.8.cloned.1.call-start = ((), (), s32[]{:S(2)}) async-start(), calls=%async_computation.3 | async-start | bytes 589824 | tf_op jit(solution)/shard_map/reduce_scatter | solution.py:183
  73.0 133.3 %copy-start.13 = (f32[128]{0:T(128)}, f32[128]{0:T(128)S(1)}, u32[]{:S(2)}) copy-start(f32[128]{0:T(128)S(1)} %convert_element_type.82) | copy-start | bytes 1540
  145.0 61.3 %copy-start.11 = (f32[128]{0:T(128)}, f32[128]{0:T(128)S(1)}, u32[]{:S(2)}) copy-start(f32[128]{0:T(128)S(1)} %add_rsqrt_fusion.2) | copy-start | bytes 1540
  222.1 47.4 %slice-start = ((f32[8,1,1024]{2,1,0:T(1,128)}), f32[1,1,1024]{2,1,0:T(1,128)S(1)}, s32[]{:S(2)}) async-start(f32[8,1,1024]{2,1,0:T(1,128)} %copy-done.2), calls=%async_computation.6 | async-start | bytes 8192 | tf_op jit(solution)/shard_map/slice | solution.py:13
  285.1 32.7 %copy-start.10 = (f32[128]{0:T(128)S(1)}, f32[128]{0:T(128)}, u32[]{:S(2)}) copy-start(f32[128]{0:T(128)} %copy-done.9) | copy-start | bytes 1540
  288.3 31.8 %copy-start.12 = (f32[128]{0:T(128)S(1)}, f32[128]{0:T(128)}, u32[]{:S(2)}) copy-start(f32[128]{0:T(128)} %copy-done.11) | copy-start | bytes 1540
  288.3 31.8 %copy-start.14 = (f32[128]{0:T(128)S(1)}, f32[128]{0:T(128)}, u32[]{:S(2)}) copy-start(f32[128]{0:T(128)} %copy-done.13) | copy-start | bytes 1540
  288.3 32.1 %copy-start.21 = (f32[128,512]{1,0:T(8,128)S(1)}, f32[128,512]{1,0:T(8,128)}, u32[]{:S(2)}) copy-start(f32[128,512]{1,0:T(8,128)} %get-tuple-element.480) | copy-start | bytes 786436
  290.4 60.3 %reduce-scatter.12.cloned.1.call-start = ((), (), s32[]{:S(2)}) async-start(), calls=%async_computation.5 | async-start | bytes 442368 | tf_op jit(solution)/shard_map/reduce_scatter | solution.py:212
  (2 other events, 16.4 us)
Sparse Core Ops, SparseCore 0:
  25.5 28.6 reduce-scatter.9
  290.5 27.2 reduce-scatter.7
  321.7 28.8 reduce-scatter.11
